TPU v7x, 256 devices: a whole 4x4x8 slice. The times are simulated.
256 devices in a mesh: mom: 64 (over x, y, z_lo, core), spin: 4 (over z_hi).
Axes of the slice: x: 4, y: 4, z: 8 (z_hi: 4, z_lo: 2; z = z_hi * 2 + z_lo), core: 2. Of those that a mesh axis runs over, the one named last changes fastest.
Arguments:
- vertex_start: bfloat16 [64, 4, 768, 768], P('mom', 'spin'), may hold values from -6 to 6
- bare_vertex: bfloat16 [64, 4, 768, 768], P('mom', 'spin'), may hold values from -6 to 6
- bubble: bfloat16 [64, 4, 64, 12, 12], P('mom', 'spin'), may hold values from -0.011962891 to 0.011962891
- form_mix: bfloat16 [2, 12, 12], replicated, may hold values from -0.59765625 to 0.59765625
- cross_tables: int32 [2, 64, 64], replicated, may hold values from 0 to 63, as said below
- freq_perm: int32 [2, 64], replicated, may hold values from 0 to 63, each once within a row
Outputs:
- vertex_final: bfloat16 [64, 4, 768, 768], P('mom', 'spin')
Inputs may be any that keep to these rules, and one draw needn't show every extreme that they name: `cross_tables`: for each crossing and frequency, the entries over the 64 momenta are a permutation of the momenta; for each crossing and momentum, every momentum appears exactly once over the 64 frequencies.
All inputs are finite; a program needn't handle non-finite values.
Results may differ from a plain program's by a relative error of at most 0.0085.
Values may be sent and summed in bfloat16 or wider, within the bound.
No kernel may reach another device: no remote copies, remote signals or barrier semaphores. Data moves between devices by JAX's collectives and lax.ppermute only.
A program may use at most 64 MiB of HBM per device.

v0:
```python
import jax
import jax.numpy as jnp
from jax import lax
from jax.sharding import PartitionSpec as P

INNER = 2
COEF_SELF = (-0.5, 0.5, 0.5, 0.5)
COEF_PAIR = (-1.5, -0.5, 1.5, -0.5)


def partner_2(value, axis, stride):
    mask = 2**stride
    pairs = [(source, source ^ mask) for source in range(lax.axis_size(axis))]
    return lax.ppermute(value, axis, pairs)


def make_orders(table, frequency_perm, momentum, momenta, per_peer, freqs):
    freq_range = jnp.arange(freqs, dtype=jnp.int32)
    own_row = jnp.take(table, momentum, axis=0)
    send_order = jnp.argsort(own_row * freqs + freq_range)
    hit_mask = (table == momentum).astype(jnp.int32)
    source = jnp.sum(hit_mask * jnp.arange(momenta, dtype=jnp.int32)[:, None], axis=0)
    within = jnp.sum(hit_mask * (jnp.cumsum(hit_mask, axis=1) - 1), axis=0)
    position = source * per_peer + within
    freq_of = jnp.argsort(frequency_perm)
    return (send_order, jnp.take(position, freq_of, axis=0))


def pack_blocks(matrix, send_order, momenta, per_peer, freqs, forms):
    order_len = matrix.shape[1]
    blocks = jnp.take(matrix.reshape(freqs, forms, order_len), send_order, axis=0)
    return blocks.reshape(momenta, per_peer, forms, order_len)


def unpack_blocks(received, recv_order, mixing, freqs, forms):
    order_len = received.shape[-1]
    gathered = jnp.take(received.reshape(freqs, forms, order_len), recv_order, axis=0)
    mixed = jnp.einsum("lm,fmb->flb", mixing, gathered, preferred_element_type=jnp.float32)
    return mixed.reshape(freqs * forms, order_len)


def local(vertex_start, bare_vertex, bubble, form_mix, cross_tables, freq_perm):
    current = vertex_start[0, 0]
    bare_mat = bare_vertex[0, 0]
    bubble_mat = bubble[0, 0]
    freqs, forms = (bubble_mat.shape[0], bubble_mat.shape[1])
    order_len = current.shape[0]
    momenta = lax.axis_size("mom")
    per_peer = freqs // momenta
    momentum = lax.axis_index("mom")
    channel = lax.axis_index("spin")
    coef_self = jnp.take(jnp.array(COEF_SELF, jnp.float32), channel)
    coef_pair = jnp.take(jnp.array(COEF_PAIR, jnp.float32), channel)
    orders_first = make_orders(cross_tables[0], freq_perm[0], momentum, momenta, per_peer, freqs)
    orders_second = make_orders(cross_tables[1], freq_perm[1], momentum, momenta, per_peer, freqs)
    partner = partner_2(current, "spin", 0)
    stacked = jnp.stack(
        [
            pack_blocks(current, orders_first[0], momenta, per_peer, freqs, forms),
            pack_blocks(partner, orders_first[0], momenta, per_peer, freqs, forms),
            pack_blocks(current, orders_second[0], momenta, per_peer, freqs, forms),
            pack_blocks(partner, orders_second[0], momenta, per_peer, freqs, forms),
        ]
    )
    received = lax.all_to_all(stacked, "mom", split_axis=1, concat_axis=1, tiled=True)
    own_sum = unpack_blocks(received[0], orders_first[1], form_mix[0], freqs, forms)
    own_sum = own_sum + unpack_blocks(received[2], orders_second[1], form_mix[1], freqs, forms)
    other_sum = unpack_blocks(received[1], orders_first[1], form_mix[0], freqs, forms)
    other_sum = other_sum + unpack_blocks(received[3], orders_second[1], form_mix[1], freqs, forms)
    own_round = own_sum.astype(jnp.bfloat16)
    other_round = other_sum.astype(jnp.bfloat16)
    reducible = (
        coef_self * own_round.astype(jnp.float32) + coef_pair * other_round.astype(jnp.float32)
    ).astype(jnp.bfloat16)
    base_sum = bare_mat.astype(jnp.float32) + reducible.astype(jnp.float32)
    for inner_step in range(INNER):
        carried = jnp.einsum(
            "fln,fnb->flb",
            bubble_mat,
            current.reshape(freqs, forms, order_len),
            preferred_element_type=jnp.float32,
        )
        carried = carried.reshape(order_len, order_len).astype(jnp.bfloat16)
        total = base_sum + jnp.dot(bare_mat, carried, preferred_element_type=jnp.float32)
        total = total + jnp.dot(reducible, carried, preferred_element_type=jnp.float32)
        current = total.astype(jnp.bfloat16)
    return current[None, None]


def solution(mesh):
    in_specs = (
        P("mom", "spin", None, None),
        P("mom", "spin", None, None),
        P("mom", "spin", None, None, None),
        P(),
        P(),
        P(),
    )
    out_specs = P("mom", "spin", None, None)
    return jax.shard_map(local, mesh=mesh, in_specs=in_specs, out_specs=out_specs, check_vma=False)
```

profile of v0, /device:TPU:240, one launch (start us, length us, event | category | flops | bytes accessed | tf_op | source)
XLA Modules:
  0.0 203.2 jit_solution(17556819864388075838)
XLA Ops:
  1.5 2.2 %reshape_squeeze.17 = bf16[64,12,768]{2,1,0:T(8,128)(2,1)S(1)} reshape(bf16[1,1,768,768]{3,2,1,0:T(8,128)(2,1)} %param.14) | data formatting | bytes 2359296 | tf_op jit(solution)/shard_map/reshape;squeeze | solution.py:31
  3.7 2.0 %sort.60 = (s32[64]{0:T(128)}, s32[64]{0:T(128)S(1)}) sort(s32[64]{0:T(128)S(1)} %fusion.29, s32[64]{0:T(128)S(1)} %iota.27), dimensions={0}, to_apply=%region_1.0 | sort | flops 384 | bytes 1024 | tf_op jit(solution)/shard_map/jit(argsort)/sort | solution.py:20
  5.8 2.0 %sort.59 = (s32[64]{0:T(128)}, s32[64]{0:T(128)S(1)}) sort(s32[64]{0:T(128)S(1)} %fusion.26, s32[64]{0:T(128)S(1)} %iota.25), dimensions={0}, to_apply=%region_0.0 | sort | flops 384 | bytes 1024 | tf_op jit(solution)/shard_map/jit(argsort)/sort | solution.py:20
  7.8 1.8 gather_fusion.2
  9.6 1.8 gather_fusion
  11.4 42.8 %collective-permute-done = bf16[768,768]{1,0:T(8,128)(2,1)} collective-permute-done((bf16[768,768]{1,0:T(8,128)(2,1)}, bf16[768,768]{1,0:T(8,128)(2,1)}, u32[]{:S(2)}, u32[]{:S(2)}) %collective-permute-start) | collective-permute-done | bytes 1179680 | tf_op jit(solution)/shard_map/ppermute | solution.py:14
  54.2 2.2 %reshape.41 = bf16[64,12,768]{2,1,0:T(8,128)(2,1)S(1)} reshape(bf16[768,768]{1,0:T(8,128)(2,1)} %collective-permute-done) | data formatting | bytes 2359296 | tf_op jit(solution)/shard_map/reshape | solution.py:31
  56.4 1.8 gather_fusion.1
  58.2 1.8 gather_fusion.3
  60.0 2.4 %select_bitcast_fusion.1 = (bf16[1,64,1,12,768]{4,3,1,2,0:T(8,128)(2,1)S(1)}, bf16[1,64,1,12,768]{4,3,1,2,0:T(8,128)(2,1)S(1)}) fusion(bf16[64,12,768]{2,1,0:T(8,128)(2,1)} %gather_fusion.2, pred[64]{0:T(512)(128)(4,1)S(1)} %get-tuple-element.99, bf16[64,12,768]{2,1,0:T(8,128)(2,1)} %gather_fusion.3), kind=kLoop, calls=%fused_computation.35 | loop fusion | flops 1179648 | bytes 4718656 | tf_op jit(solution)/shard_map/stack;reshape | solution.py:57
  64.3 8.2 %copy.39 = bf16[4,64,1,12,768]{4,0,3,2,1:T(4,128)(2,1)} copy(bf16[4,64,1,12,768]{4,3,1,2,0:T(8,128)(2,1)S(1)} %pad_maximum_fusion) | data formatting | bytes 9437184 | tf_op jit(solution)/shard_map/stack | solution.py:57
  72.5 9.0 %all-to-all-start = ((bf16[4,64,1,12,768]{4,0,3,2,1:T(4,128)(2,1)}), bf16[4,64,1,12,768]{4,0,3,2,1:T(4,128)(2,1)}, u32[]{:S(2)}, u32[]{:S(2)}) async-start(bf16[4,64,1,12,768]{4,0,3,2,1:T(4,128)(2,1)} %copy.39), calls=%async_computation | async-start | bytes 9437184 | tf_op jit(solution)/shard_map/all_to_all | solution.py:65
  86.7 2.0 %sort.62 = (s32[64]{0:T(128)}, s32[64]{0:T(128)S(1)}) sort(s32[64]{0:T(128)S(1)} %get-tuple-element.89, s32[64]{0:T(128)S(1)} %iota.29), dimensions={0}, to_apply=%region_9.13 | sort | flops 384 | bytes 1024 | tf_op jit(solution)/shard_map/jit(argsort)/sort | solution.py:25
  88.7 2.0 %sort.61 = (s32[64]{0:T(128)}, s32[64]{0:T(128)S(1)}) sort(s32[64]{0:T(128)S(1)} %get-tuple-element.90, s32[64]{0:T(128)S(1)} %iota.28), dimensions={0}, to_apply=%region_5.8 | sort | flops 384 | bytes 1024 | tf_op jit(solution)/shard_map/jit(argsort)/sort | solution.py:25
  92.5 52.2 %all-to-all-done = bf16[4,64,1,12,768]{4,0,3,2,1:T(4,128)(2,1)} async-done(((bf16[4,64,1,12,768]{4,0,3,2,1:T(4,128)(2,1)}), bf16[4,64,1,12,768]{4,0,3,2,1:T(4,128)(2,1)}, u32[]{:S(2)}, u32[]{:S(2)}) %all-to-all-start) | async-done | bytes 4718624 | tf_op jit(solution)/shard_map/all_to_all | solution.py:65
  144.6 15.4 %fusion.36 = (bf16[1,64,1,12,768]{4,0,3,2,1:T(2,128)(2,1)S(1)}, bf16[1,64,1,12,768]{4,0,3,2,1:T(2,128)(2,1)S(1)}, bf16[1,64,1,12,768]{4,0,3,2,1:T(2,128)(2,1)S(1)}, bf16[1,64,1,12,768]{4,0,3,2,1:T(2,128)(2,1)}) fusion(bf16[4,64,1,12,768]{4,0,3,2,1:T(4,128)(2,1)} %all-to-all-done), kind=kLoop, calls=%fused_computation.94 | loop fusion | bytes 9437184 | tf_op jit(solution)/shard_map/slice | solution.py:67
  160.0 1.5 copy.76
  162.2 1.8 gather_fusion.8
  164.0 1.8 gather_fusion.5
  165.8 2.2 %fusion.5 = f32[64,768,12]{1,2,0:T(8,128)S(1)} fusion(bf16[64,12,768]{2,1,0:T(8,128)(2,1)} %gather_fusion.8, pred[64]{0:T(512)(128)(4,1)S(1)} %get-tuple-element.75, bf16[1,12,12]{2,0,1:T(2,128)(2,1)S(1)} %get-tuple-element.88), kind=kOutput, calls=%fused_computation.29 | convolution fusion | flops 14745600 | bytes 3539296 | tf_op jit(solution)/shard_map/lm,fmb->flb/dot_general | solution.py:38
  168.0 2.3 %fusion.8 = f32[64,768,12]{1,2,0:T(8,128)} fusion(bf16[64,12,768]{2,1,0:T(8,128)(2,1)S(1)} %copy-done.4, pred[64]{0:T(512)(128)(4,1)S(1)} %get-tuple-element.75, bf16[1,12,12]{2,0,1:T(2,128)(2,1)S(1)} %get-tuple-element.88), kind=kOutput, calls=%fused_computation.32 | convolution fusion | flops 14745600 | bytes 3539296 | tf_op jit(solution)/shard_map/lm,fmb->flb/dot_general | solution.py:38
  170.3 1.5 copy.74
  171.8 3.2 %gather_fusion.7 = bf16[64,12,768]{2,1,0:T(8,128)(2,1)} fusion(bf16[64,12,768]{2,1,0:T(8,128)(2,1)} %bitcast.104, s32[1024]{0:T(1024)S(1)} %pad_clamp_fusion), kind=kCustom, calls=%fused_computation.6.clone | custom fusion | bytes 2359552 | tf_op jit(solution)/shard_map/jit(_take)/gather | solution.py:37
  175.1 3.2 %gather_fusion.9 = bf16[64,12,768]{2,1,0:T(8,128)(2,1)} fusion(bf16[64,12,768]{2,1,0:T(8,128)(2,1)} %bitcast.106, s32[1024]{0:T(1024)S(1)} %pad_clamp_fusion), kind=kCustom, calls=%fused_computation.8.clone | custom fusion | bytes 2359552 | tf_op jit(solution)/shard_map/jit(_take)/gather | solution.py:37
  178.3 2.2 %add_convert_fusion.1 = bf16[64,768,12]{1,2,0:T(8,128)(2,1)S(1)} fusion(f32[64,768,12]{1,2,0:T(8,128)S(1)} %fusion.5, bf16[64,12,768]{2,1,0:T(8,128)(2,1)} %gather_fusion.9, pred[64]{0:T(512)(128)(4,1)S(1)} %get-tuple-element.71, bf16[1,12,12]{2,0,1:T(2,128)(2,1)S(1)} %get-tuple-element.87), kind=kOutput, calls=%fused_computation.13 | convolution fusion | flops 15925248 | bytes 4718944 | tf_op jit(solution)/shard_map/lm,fmb->flb/dot_general | solution.py:38
  182.2 2.1 %convert_bitcast_fusion = f32[64,12,768]{2,1,0:T(8,128)} fusion(bf16[64,768,12]{1,2,0:T(8,128)(2,1)S(1)} %add_convert_fusion), kind=kLoop, calls=%fused_computation.11 | loop fusion | flops 589824 | bytes 3538944 | tf_op jit(solution)/shard_map/convert_element_type | solution.py:75
  185.4 2.6 %reshape.145 = f32[768,768]{1,0:T(8,128)S(1)} reshape(f32[64,12,768]{2,1,0:T(8,128)} %convert_bitcast_fusion) | data formatting | bytes 4718592 | tf_op jit(solution)/shard_map/convert_element_type | solution.py:75
  188.1 3.6 %fusion.38 = f32[768,768]{1,0:T(8,128)S(1)} fusion(bf16[768,768]{1,0:T(8,128)(2,1)} %convert_element_type.94, bf16[768,768]{1,0:T(8,128)(2,1)} %convert_element_type.92), kind=kOutput, calls=%fused_computation.96 | convolution fusion | flops 905969664 | bytes 4718592 | tf_op jit(solution)/shard_map/dot_general | solution.py:85
  191.7 2.2 %fusion.3 = bf16[768,768]{1,0:T(8,128)(2,1)} fusion(f32[768,768]{1,0:T(8,128)S(1)} %fusion.38, bf16[768,768]{1,0:T(8,128)(2,1)S(1)} %copy-done.8, f32[768,768]{1,0:T(8,128)S(1)} %reshape.145, bf16[1,1,768,768]{3,2,1,0:T(8,128)(2,1)S(1)} %copy-done.15), kind=kOutput, calls=%fused_computation.20 | convolution fusion | flops 908918784 | bytes 8257536 | tf_op jit(solution)/shard_map/dot_general | solution.py:84
  193.9 2.2 %reshape.42 = bf16[64,12,768]{2,1,0:T(8,128)(2,1)S(1)} reshape(bf16[768,768]{1,0:T(8,128)(2,1)} %fusion.3) | data formatting | bytes 2359296 | tf_op jit(solution)/shard_map/reshape | solution.py:80
  198.4 2.5 %fusion.39 = f32[768,768]{1,0:T(8,128)S(1)} fusion(bf16[768,768]{1,0:T(8,128)(2,1)S(1)} %copy-done.9, bf16[768,768]{1,0:T(8,128)(2,1)} %convert_element_type.98), kind=kOutput, calls=%fused_computation.97 | convolution fusion | flops 905969664 | bytes 4718592 | tf_op jit(solution)/shard_map/dot_general | solution.py:85
  201.0 2.2 %fusion.15 = bf16[1,1,768,768]{3,2,1,0:T(8,128)(2,1)} fusion(f32[768,768]{1,0:T(8,128)S(1)} %fusion.39, bf16[768,768]{1,0:T(8,128)(2,1)S(1)} %copy-done.10, f32[768,768]{1,0:T(8,128)S(1)} %copy-done.7, bf16[1,1,768,768]{3,2,1,0:T(8,128)(2,1)S(1)} %copy-done.16), kind=kOutput, calls=%fused_computation.43 | convolution fusion | flops 908918784 | bytes 8257536 | tf_op jit(solution)/shard_map/dot_general | solution.py:84
  (80 shorter events, 14.7 us)
Async XLA Ops:
  0.0 3.7 %copy-start.11 = (s32[2,64,64]{2,1,0:T(8,128)S(1)}, s32[2,64,64]{2,1,0:T(8,128)}, u32[]{:S(2)}) copy-start(s32[2,64,64]{2,1,0:T(8,128)} %param.18) | copy-start | bytes 98308
  0.0 54.2 %collective-permute-start = (bf16[768,768]{1,0:T(8,128)(2,1)}, bf16[768,768]{1,0:T(8,128)(2,1)}, u32[]{:S(2)}, u32[]{:S(2)}) collective-permute-start(bf16[768,768]{1,0:T(8,128)(2,1)} %bitcast.108), channel_id=1, source_target_pairs={{0,1},{1,0},{2,3},{3,2},{4,5},{5,4},{6,7},{7,6},{8,9},{9,8},{10,11... | collective-permute-start | bytes 3538952 | tf_op jit(solution)/shard_map/ppermute | solution.py:14
  60.0 2.4 %copy-start.2 = (bf16[64,12,768]{2,1,0:T(8,128)(2,1)S(1)}, bf16[64,12,768]{2,1,0:T(8,128)(2,1)}, u32[]{:S(2)}) copy-start(bf16[64,12,768]{2,1,0:T(8,128)(2,1)} %gather_fusion) | copy-start | bytes 3538948
  60.0 2.8 %copy-start.3 = (bf16[64,12,768]{2,1,0:T(8,128)(2,1)S(1)}, bf16[64,12,768]{2,1,0:T(8,128)(2,1)}, u32[]{:S(2)}) copy-start(bf16[64,12,768]{2,1,0:T(8,128)(2,1)} %gather_fusion.1) | copy-start | bytes 3538948
  72.5 9.1 %copy-start.18 = (f32[4]{0:T(128)S(1)}, f32[4]{0:T(128)}, u32[]{:S(2)}) copy-start(f32[4]{0:T(128)} %constant.83.clone..sunk.2) | copy-start | bytes 52
  72.5 9.7 %copy-start.17 = (f32[4]{0:T(128)S(1)}, f32[4]{0:T(128)}, u32[]{:S(2)}) copy-start(f32[4]{0:T(128)} %constant.82.clone..sunk.2) | copy-start | bytes 52
  72.5 12.1 %copy-start.12 = (bf16[1,1,64,12,12]{2,4,3,1,0:T(8,128)(2,1)S(1)}, bf16[1,1,64,12,12]{2,4,3,1,0:T(8,128)(2,1)}, u32[]{:S(2)}) copy-start(bf16[1,1,64,12,12]{2,4,3,1,0:T(8,128)(2,1)} %param.16) | copy-start | bytes 55300
  72.5 72.1 %all-to-all-start = ((bf16[4,64,1,12,768]{4,0,3,2,1:T(4,128)(2,1)}), bf16[4,64,1,12,768]{4,0,3,2,1:T(4,128)(2,1)}, u32[]{:S(2)}, u32[]{:S(2)}) async-start(bf16[4,64,1,12,768]{4,0,3,2,1:T(4,128)(2,1)} %copy.39), calls=%async_computation | async-start | bytes 9437184 | tf_op jit(solution)/shard_map/all_to_all | solution.py:65
  85.5 1.2 copy-start.14
  85.5 7.0 %copy-start.13 = (bf16[2,12,12]{2,0,1:T(2,128)(2,1)S(1)}, bf16[2,12,12]{2,0,1:T(2,128)(2,1)}, u32[]{:S(2)}) copy-start(bf16[2,12,12]{2,0,1:T(2,128)(2,1)} %param.17) | copy-start | bytes 1732
  165.8 2.2 %copy-start.4 = (bf16[64,12,768]{2,1,0:T(8,128)(2,1)S(1)}, bf16[64,12,768]{2,1,0:T(8,128)(2,1)}, u32[]{:S(2)}) copy-start(bf16[64,12,768]{2,1,0:T(8,128)(2,1)} %gather_fusion.5) | copy-start | bytes 3538948
  168.0 2.3 %copy-start.1 = (bf16[1,64,1,12,768]{4,0,3,2,1:T(2,128)(2,1)S(1)}, bf16[1,64,1,12,768]{4,0,3,2,1:T(2,128)(2,1)}, u32[]{:S(2)}) copy-start(bf16[1,64,1,12,768]{4,0,3,2,1:T(2,128)(2,1)} %get-tuple-element.82) | copy-start | bytes 3538948
  178.3 2.4 %copy-start = (f32[64,768,12]{1,2,0:T(8,128)S(1)}, f32[64,768,12]{1,2,0:T(8,128)}, u32[]{:S(2)}) copy-start(f32[64,768,12]{1,2,0:T(8,128)} %fusion.8) | copy-start | bytes 7077892
  178.3 2.8 %copy-start.5 = (bf16[64,12,768]{2,1,0:T(8,128)(2,1)S(1)}, bf16[64,12,768]{2,1,0:T(8,128)(2,1)}, u32[]{:S(2)}) copy-start(bf16[64,12,768]{2,1,0:T(8,128)(2,1)} %gather_fusion.7) | copy-start | bytes 3538948
  188.0 3.6 %copy-start.6 = (f32[768,768]{1,0:T(8,128)}, f32[768,768]{1,0:T(8,128)S(1)}, u32[]{:S(2)}) copy-start(f32[768,768]{1,0:T(8,128)S(1)} %reshape.145) | copy-start | bytes 7077892
  188.0 3.6 %copy-start.8 = (bf16[768,768]{1,0:T(8,128)(2,1)S(1)}, bf16[768,768]{1,0:T(8,128)(2,1)}, u32[]{:S(2)}) copy-start(bf16[768,768]{1,0:T(8,128)(2,1)} %convert_element_type.92) | copy-start | bytes 3538948
  188.1 3.6 %copy-start.15 = (bf16[1,1,768,768]{3,2,1,0:T(8,128)(2,1)S(1)}, bf16[1,1,768,768]{3,2,1,0:T(8,128)(2,1)}, u32[]{:S(2)}) copy-start(bf16[1,1,768,768]{3,2,1,0:T(8,128)(2,1)} %param.15) | copy-start | bytes 3538948
  196.7 1.7 copy-start.9
  198.4 2.5 %copy-start.7 = (f32[768,768]{1,0:T(8,128)S(1)}, f32[768,768]{1,0:T(8,128)}, u32[]{:S(2)}) copy-start(f32[768,768]{1,0:T(8,128)} %copy-done.6) | copy-start | bytes 7077892
  198.4 2.5 %copy-start.10 = (bf16[768,768]{1,0:T(8,128)(2,1)S(1)}, bf16[768,768]{1,0:T(8,128)(2,1)}, u32[]{:S(2)}) copy-start(bf16[768,768]{1,0:T(8,128)(2,1)} %convert_element_type.98) | copy-start | bytes 3538948
  198.4 2.7 %copy-start.16 = (bf16[1,1,768,768]{3,2,1,0:T(8,128)(2,1)S(1)}, bf16[1,1,768,768]{3,2,1,0:T(8,128)(2,1)}, u32[]{:S(2)}) copy-start(bf16[1,1,768,768]{3,2,1,0:T(8,128)(2,1)} %param.15) | copy-start | bytes 3538948
where the time goes:
time: 204 us; the launch traced here: 203 us
  waiting for transfers between devices  95 us (47%)
  local copies, waits for them, and re-layouts  62 us (30%)
  matrix products  19.4 us (10%)
  other arithmetic  14.7 us (7%)
  starting transfers between devices  10.5 us (5%)
    all_to_all x1, waiting for transfers between devices, local(): lax.all_to_all(stacked, 'mom', split_axis=1, concat_axis=1, tiled=True)  52.2 us
    ppermute x1, waiting for transfers between devices, partner_2(): return lax.ppermute(value, axis, pairs)  42.8 us
    slice x1, local copies, waits for them, and re-layouts, local(): received[2]  15.4 us
    gather x4, local copies, waits for them, and re-layouts, unpack_blocks(): jnp.take(received.reshape(freqs, forms, order_len), recv_order, axis=0)  10 us
    all_to_all x1, starting transfers between devices, local(): lax.all_to_all(stacked, 'mom', split_axis=1, concat_axis=1, tiled=True)  9.03 us
    another operation x1, local copies, waits for them, and re-layouts, local(): jnp.stack([pack_blocks(current, orders_first[0], momenta, per_peer, freqs...  8.24 us
    dot_general x4, matrix products, unpack_blocks(): jnp.einsum('lm,fmb->flb', mixing, gathered, preferred_element_type=jnp.fl...  7.81 us
    gather x4, local copies, waits for them, and re-layouts, pack_blocks(): jnp.take(matrix.reshape(freqs, forms, order_len), send_order, axis=0)  7.2 us
  transfers between devices with their start and end apart: 2, of which 2 were waited for; matrix products, arithmetic and copies ran while one was open for 10% of the time, Pallas kernels for 0%

commit v1 on v0

--- a/solution.py
+++ b/solution.py
@@ -62,7 +62,9 @@
             pack_blocks(partner, orders_second[0], momenta, per_peer, freqs, forms),
         ]
     )
-    received = lax.all_to_all(stacked, "mom", split_axis=1, concat_axis=1, tiled=True)
+    parts = jnp.split(stacked, lax.axis_size("mom"), axis=1)
+    incoming = lax.all_to_all(jnp.stack(parts), "mom", 0, 0)
+    received = jnp.concatenate(incoming, axis=1)
     own_sum = unpack_blocks(received[0], orders_first[1], form_mix[0], freqs, forms)
     own_sum = own_sum + unpack_blocks(received[2], orders_second[1], form_mix[1], freqs, forms)
     other_sum = unpack_blocks(received[1], orders_first[1], form_mix[0], freqs, forms)

time: 204 us -> 185 us (0.907)
  local copies, waits for them, and re-layouts: 62 us -> 48.1 us
  matrix products: 19.4 us -> 15.1 us
    slice x1 -> x0, local copies, waits for them, and re-layouts: 15.4 us -> none  [local(): received[2]]
    another operation x4 -> x5, local copies, waits for them, and re-layouts: 3.71 us -> 8.14 us  [unpack_blocks(): received.reshape(freqs, forms, order_len)]
    all_to_all x0 -> x1, local copies, waits for them, and re-layouts: none -> 3.91 us  [local(): incoming = lax.all_to_all(jnp.stack(parts), 'mom', 0, 0)]
    gather x4, local copies, waits for them, and re-layouts: 10 us -> 6.28 us  [unpack_blocks(): jnp.take(received.reshape(freqs, forms, order_len), recv_order, axis=0)]
    another operation x1 -> x2, local copies, waits for them, and re-layouts: 8.24 us -> 4.61 us  [local(): incoming = lax.all_to_all(jnp.stack(parts), 'mom', 0, 0)]
    dot_general x4, matrix products: 7.81 us -> 4.57 us  [unpack_blocks(): jnp.einsum('lm,fmb->flb', mixing, gathered, preferred_element_type=jnp.fl...]
  transfers between devices with their start and end apart: 2 -> 2, of which waited for: 2 -> 2; matrix products, arithmetic and copies ran while one was open for 10% -> 11% of each run, Pallas kernels for 0% -> 0%
where the time goes in v1:
time: 185 us
  waiting for transfers between devices  94.2 us (51%)
  local copies, waits for them, and re-layouts  48.1 us (26%)
  matrix products  15.1 us (8%)
  other arithmetic  14.7 us (8%)
  starting transfers between devices  10.5 us (6%)
  between operations  2.22 us (1%)
    all_to_all x1, waiting for transfers between devices, local(): incoming = lax.all_to_all(jnp.stack(parts), 'mom', 0, 0)  52.2 us
    ppermute x1, waiting for transfers between devices, partner_2(): return lax.ppermute(value, axis, pairs)  42 us
    all_to_all x1, starting transfers between devices, local(): incoming = lax.all_to_all(jnp.stack(parts), 'mom', 0, 0)  9.05 us
    another operation x5, local copies, waits for them, and re-layouts, unpack_blocks(): received.reshape(freqs, forms, order_len)  8.14 us
    gather x4, local copies, waits for them, and re-layouts, pack_blocks(): jnp.take(matrix.reshape(freqs, forms, order_len), send_order, axis=0)  7.2 us
    gather x4, local copies, waits for them, and re-layouts, unpack_blocks(): jnp.take(received.reshape(freqs, forms, order_len), recv_order, axis=0)  6.28 us
    dot_general x2, matrix products, local(): jnp.dot(reducible, carried, preferred_element_type=jnp.float32)  5.02 us
    another operation x2, local copies, waits for them, and re-layouts, local(): incoming = lax.all_to_all(jnp.stack(parts), 'mom', 0, 0)  4.61 us
  transfers between devices with their start and end apart: 2, of which 2 were waited for; matrix products, arithmetic and copies ran while one was open for 11% of the time, Pallas kernels for 0%

profile of v1, /device:TPU:240, one launch (start us, length us, event | category | flops | bytes accessed | tf_op | source)
XLA Modules:
  0.0 184.8 jit_solution(17708618855114819446)
XLA Ops:
  0.0 1.5 collective-permute-start
  1.5 2.2 %reshape_squeeze.17 = bf16[64,12,768]{2,1,0:T(8,128)(2,1)S(1)} reshape(bf16[1,1,768,768]{3,2,1,0:T(8,128)(2,1)} %param.14) | data formatting | bytes 2359296 | tf_op jit(solution)/shard_map/reshape;squeeze | solution.py:31
  4.5 2.0 %sort.60 = (s32[64]{0:T(128)}, s32[64]{0:T(128)S(1)}) sort(s32[64]{0:T(128)S(1)} %fusion.29, s32[64]{0:T(128)S(1)} %iota.27), dimensions={0}, to_apply=%region_1.0 | sort | flops 384 | bytes 1024 | tf_op jit(solution)/shard_map/jit(argsort)/sort | solution.py:20
  6.5 2.0 %sort.59 = (s32[64]{0:T(128)}, s32[64]{0:T(128)S(1)}) sort(s32[64]{0:T(128)S(1)} %fusion.26, s32[64]{0:T(128)S(1)} %iota.25), dimensions={0}, to_apply=%region_0.0 | sort | flops 384 | bytes 1024 | tf_op jit(solution)/shard_map/jit(argsort)/sort | solution.py:20
  8.6 1.8 gather_fusion.2
  10.4 1.8 gather_fusion
  12.2 42.0 %collective-permute-done = bf16[768,768]{1,0:T(8,128)(2,1)} collective-permute-done((bf16[768,768]{1,0:T(8,128)(2,1)}, bf16[768,768]{1,0:T(8,128)(2,1)}, u32[]{:S(2)}, u32[]{:S(2)}) %collective-permute-start) | collective-permute-done | bytes 1179680 | tf_op jit(solution)/shard_map/ppermute | solution.py:14
  54.2 2.2 %reshape.53 = bf16[64,12,768]{2,1,0:T(8,128)(2,1)S(1)} reshape(bf16[768,768]{1,0:T(8,128)(2,1)} %collective-permute-done) | data formatting | bytes 2359296 | tf_op jit(solution)/shard_map/reshape | solution.py:31
  56.4 1.8 gather_fusion.1
  58.2 1.8 gather_fusion.3
  60.0 2.4 %select_bitcast_fusion.1 = (bf16[1,64,1,12,768]{4,3,1,2,0:T(8,128)(2,1)S(1)}, bf16[1,64,1,12,768]{4,3,1,2,0:T(8,128)(2,1)S(1)}) fusion(bf16[64,12,768]{2,1,0:T(8,128)(2,1)} %gather_fusion.2, pred[64]{0:T(512)(128)(4,1)S(1)} %get-tuple-element.99, bf16[64,12,768]{2,1,0:T(8,128)(2,1)} %gather_fusion.3), kind=kLoop, calls=%fused_computation.32 | loop fusion | flops 1179648 | bytes 4718656 | tf_op jit(solution)/shard_map/stack;reshape | solution.py:57
  65.4 4.6 %copy.351 = bf16[64,4,1,1,12,768]{5,1,4,3,2,0:T(4,128)(2,1)} copy(bf16[64,4,1,1,12,768]{5,4,1,3,2,0:T(8,128)(2,1)S(1)} %constant_dynamic-update-slice_fusion) | data formatting | bytes 9437184 | tf_op jit(solution)/shard_map/stack | solution.py:66
  70.0 9.0 %all-to-all-start = ((bf16[64,4,1,1,12,768]{5,1,4,3,2,0:T(4,128)(2,1)}), bf16[64,4,1,1,12,768]{5,1,4,3,2,0:T(4,128)(2,1)}, u32[]{:S(2)}, u32[]{:S(2)}) async-start(bf16[64,4,1,1,12,768]{5,1,4,3,2,0:T(4,128)(2,1)} %copy.351), calls=%async_computation | async-start | bytes 9437184 | tf_op jit(solution)/shard_map/all_to_all | solution.py:66
  83.0 1.2 convert_element_type.92
  84.1 2.0 %sort.62 = (s32[64]{0:T(128)}, s32[64]{0:T(128)S(1)}) sort(s32[64]{0:T(128)S(1)} %get-tuple-element.89, s32[64]{0:T(128)S(1)} %iota.29), dimensions={0}, to_apply=%region_9.13 | sort | flops 384 | bytes 1024 | tf_op jit(solution)/shard_map/jit(argsort)/sort | solution.py:25
  86.2 2.0 %sort.61 = (s32[64]{0:T(128)}, s32[64]{0:T(128)S(1)}) sort(s32[64]{0:T(128)S(1)} %get-tuple-element.90, s32[64]{0:T(128)S(1)} %iota.28), dimensions={0}, to_apply=%region_5.8 | sort | flops 384 | bytes 1024 | tf_op jit(solution)/shard_map/jit(argsort)/sort | solution.py:25
  89.9 52.2 %all-to-all-done = bf16[64,4,1,1,12,768]{5,1,4,3,2,0:T(4,128)(2,1)} async-done(((bf16[64,4,1,1,12,768]{5,1,4,3,2,0:T(4,128)(2,1)}), bf16[64,4,1,1,12,768]{5,1,4,3,2,0:T(4,128)(2,1)}, u32[]{:S(2)}, u32[]{:S(2)}) %all-to-all-start) | async-done | bytes 4718624 | tf_op jit(solution)/shard_map/all_to_all | solution.py:66
  142.1 3.9 %copy.435 = bf16[64,4,1,1,12,768]{5,0,4,3,2,1:T(8,128)(2,1)S(1)} copy(bf16[64,4,1,1,12,768]{5,1,4,3,2,0:T(4,128)(2,1)} %all-to-all-done) | data formatting | bytes 9437184 | tf_op jit(solution)/shard_map/all_to_all | solution.py:66
  146.0 1.8 slice_bitcast_fusion.2
  149.2 1.8 gather_fusion.7
  151.6 1.9 %copy.357 = bf16[64,12,768]{2,1,0:T(8,128)(2,1)S(1)} copy(bf16[64,12,768]{2,0,1:T(8,128)(2,1)} %get-tuple-element.81) | data formatting | bytes 2359296 | tf_op jit(solution)/shard_map/reshape;squeeze | solution.py:37
  153.6 3.1 %copy.353 = bf16[64,12,768]{2,1,0:T(8,128)(2,1)} copy(bf16[64,12,768]{2,0,1:T(8,128)(2,1)} %get-tuple-element.82) | data formatting | bytes 2359296 | tf_op jit(solution)/shard_map/reshape;squeeze | solution.py:37
  156.6 1.8 gather_fusion.8
  158.4 2.1 %gather_fusion.5 = bf16[64,12,768]{2,1,0:T(8,128)(2,1)S(1)} fusion(bf16[64,12,768]{2,1,0:T(8,128)(2,1)} %copy.353, s32[1024]{0:T(1024)S(1)} %pad_clamp_fusion.2), kind=kCustom, calls=%fused_computation.5.clone | custom fusion | bytes 2359552 | tf_op jit(solution)/shard_map/jit(_take)/gather | solution.py:37
  160.5 2.1 %fusion.5 = f32[64,768,12]{1,2,0:T(8,128)S(1)} fusion(bf16[64,12,768]{2,1,0:T(8,128)(2,1)} %gather_fusion.8, pred[64]{0:T(512)(128)(4,1)S(1)} %get-tuple-element.75, bf16[1,12,12]{2,0,1:T(2,128)(2,1)S(1)} %get-tuple-element.88), kind=kOutput, calls=%fused_computation.26 | convolution fusion | flops 14745600 | bytes 3539296 | tf_op jit(solution)/shard_map/lm,fmb->flb/dot_general | solution.py:38
  165.1 2.1 %convert_bitcast_fusion = f32[64,12,768]{2,1,0:T(8,128)} fusion(bf16[64,768,12]{1,2,0:T(8,128)(2,1)S(1)} %add_convert_fusion), kind=kLoop, calls=%fused_computation.12 | loop fusion | flops 589824 | bytes 3538944 | tf_op jit(solution)/shard_map/convert_element_type | solution.py:77
  168.3 3.9 %reshape.158 = f32[768,768]{1,0:T(8,128)} reshape(f32[64,12,768]{2,1,0:T(8,128)} %convert_bitcast_fusion) | data formatting | bytes 4718592 | tf_op jit(solution)/shard_map/convert_element_type | solution.py:77
  172.3 2.5 %fusion.37 = f32[768,768]{1,0:T(8,128)S(1)} fusion(bf16[768,768]{1,0:T(8,128)(2,1)} %convert_element_type.94, bf16[768,768]{1,0:T(8,128)(2,1)S(1)} %copy-done.5), kind=kOutput, calls=%fused_computation.224 | convolution fusion | flops 905969664 | bytes 4718592 | tf_op jit(solution)/shard_map/dot_general | solution.py:87
  174.8 2.2 %fusion.3 = bf16[768,768]{1,0:T(8,128)(2,1)} fusion(f32[768,768]{1,0:T(8,128)S(1)} %fusion.37, bf16[768,768]{1,0:T(8,128)(2,1)S(1)} %copy-done.5, f32[768,768]{1,0:T(8,128)S(1)} %copy-done.3, bf16[1,1,768,768]{3,2,1,0:T(8,128)(2,1)S(1)} %copy-done.10), kind=kOutput, calls=%fused_computation.21 | convolution fusion | flops 908918784 | bytes 8257536 | tf_op jit(solution)/shard_map/dot_general | solution.py:86
  177.1 2.2 %reshape.55 = bf16[64,12,768]{2,1,0:T(8,128)(2,1)S(1)} reshape(bf16[768,768]{1,0:T(8,128)(2,1)} %fusion.3) | data formatting | bytes 2359296 | tf_op jit(solution)/shard_map/reshape | solution.py:82
  180.1 2.5 %fusion.38 = f32[768,768]{1,0:T(8,128)S(1)} fusion(bf16[768,768]{1,0:T(8,128)(2,1)} %convert_element_type.94, bf16[768,768]{1,0:T(8,128)(2,1)S(1)} %convert_element_type.98), kind=kOutput, calls=%fused_computation.225 | convolution fusion | flops 905969664 | bytes 4718592 | tf_op jit(solution)/shard_map/dot_general | solution.py:87
  182.7 2.2 %fusion.15 = bf16[1,1,768,768]{3,2,1,0:T(8,128)(2,1)} fusion(f32[768,768]{1,0:T(8,128)S(1)} %fusion.38, bf16[768,768]{1,0:T(8,128)(2,1)S(1)} %convert_element_type.98, f32[768,768]{1,0:T(8,128)S(1)} %copy-done.4, bf16[1,1,768,768]{3,2,1,0:T(8,128)(2,1)S(1)} %copy-done.11), kind=kOutput, calls=%fused_computation.40 | convolution fusion | flops 908918784 | bytes 8257536 | tf_op jit(solution)/shard_map/dot_general | solution.py:86
  (135 shorter events, 14.1 us)
Async XLA Ops:
  0.0 54.2 %collective-permute-start = (bf16[768,768]{1,0:T(8,128)(2,1)}, bf16[768,768]{1,0:T(8,128)(2,1)}, u32[]{:S(2)}, u32[]{:S(2)}) collective-permute-start(bf16[768,768]{1,0:T(8,128)(2,1)} %bitcast.482), channel_id=1, source_target_pairs={{0,1},{1,0},{2,3},{3,2},{4,5},{5,4},{6,7},{7,6},{8,9},{9,8},{10,11... | collective-permute-start | bytes 3538952 | tf_op jit(solution)/shard_map/ppermute | solution.py:14
  60.0 2.4 %copy-start = (bf16[64,12,768]{2,1,0:T(8,128)(2,1)S(1)}, bf16[64,12,768]{2,1,0:T(8,128)(2,1)}, u32[]{:S(2)}) copy-start(bf16[64,12,768]{2,1,0:T(8,128)(2,1)} %gather_fusion) | copy-start | bytes 3538948
  60.0 2.8 %copy-start.1 = (bf16[64,12,768]{2,1,0:T(8,128)(2,1)S(1)}, bf16[64,12,768]{2,1,0:T(8,128)(2,1)}, u32[]{:S(2)}) copy-start(bf16[64,12,768]{2,1,0:T(8,128)(2,1)} %gather_fusion.1) | copy-start | bytes 3538948
  69.9 9.1 %copy-start.13 = (f32[4]{0:T(128)S(1)}, f32[4]{0:T(128)}, u32[]{:S(2)}) copy-start(f32[4]{0:T(128)} %constant.83.clone..sunk.2) | copy-start | bytes 52
  70.0 9.7 %copy-start.12 = (f32[4]{0:T(128)S(1)}, f32[4]{0:T(128)}, u32[]{:S(2)}) copy-start(f32[4]{0:T(128)} %constant.82.clone..sunk.2) | copy-start | bytes 52
  70.0 11.7 %copy-start.6 = (s32[2,64,64]{2,1,0:T(8,128)S(1)}, s32[2,64,64]{2,1,0:T(8,128)}, u32[]{:S(2)}) copy-start(s32[2,64,64]{2,1,0:T(8,128)} %param.18) | copy-start | bytes 98308
  70.0 12.2 %copy-start.7 = (bf16[1,1,64,12,12]{2,4,3,1,0:T(8,128)(2,1)S(1)}, bf16[1,1,64,12,12]{2,4,3,1,0:T(8,128)(2,1)}, u32[]{:S(2)}) copy-start(bf16[1,1,64,12,12]{2,4,3,1,0:T(8,128)(2,1)} %param.16) | copy-start | bytes 55300
  70.0 14.2 %copy-start.9 = (s32[2,64]{1,0:T(2,128)S(1)}, s32[2,64]{1,0:T(2,128)}, u32[]{:S(2)}) copy-start(s32[2,64]{1,0:T(2,128)} %param.19) | copy-start | bytes 1540
  70.0 72.1 %all-to-all-start = ((bf16[64,4,1,1,12,768]{5,1,4,3,2,0:T(4,128)(2,1)}), bf16[64,4,1,1,12,768]{5,1,4,3,2,0:T(4,128)(2,1)}, u32[]{:S(2)}, u32[]{:S(2)}) async-start(bf16[64,4,1,1,12,768]{5,1,4,3,2,0:T(4,128)(2,1)} %copy.351), calls=%async_computation | async-start | bytes 9437184 | tf_op jit(solution)/shard_map/all_to_all | solution.py:66
  79.0 10.9 %copy-start.8 = (bf16[2,12,12]{2,0,1:T(2,128)(2,1)S(1)}, bf16[2,12,12]{2,0,1:T(2,128)(2,1)}, u32[]{:S(2)}) copy-start(bf16[2,12,12]{2,0,1:T(2,128)(2,1)} %param.17) | copy-start | bytes 1732
  162.5 1.5 copy-start.2
  165.1 7.2 %copy-start.5 = (bf16[768,768]{1,0:T(8,128)(2,1)S(1)}, bf16[768,768]{1,0:T(8,128)(2,1)}, u32[]{:S(2)}) copy-start(bf16[768,768]{1,0:T(8,128)(2,1)} %convert_element_type.92) | copy-start | bytes 3538948
  168.3 6.5 %copy-start.10 = (bf16[1,1,768,768]{3,2,1,0:T(8,128)(2,1)S(1)}, bf16[1,1,768,768]{3,2,1,0:T(8,128)(2,1)}, u32[]{:S(2)}) copy-start(bf16[1,1,768,768]{3,2,1,0:T(8,128)(2,1)} %param.15) | copy-start | bytes 3538948
  172.3 2.5 %copy-start.3 = (f32[768,768]{1,0:T(8,128)S(1)}, f32[768,768]{1,0:T(8,128)}, u32[]{:S(2)}) copy-start(f32[768,768]{1,0:T(8,128)} %reshape.158) | copy-start | bytes 7077892
  180.1 2.5 %copy-start.4 = (f32[768,768]{1,0:T(8,128)S(1)}, f32[768,768]{1,0:T(8,128)}, u32[]{:S(2)}) copy-start(f32[768,768]{1,0:T(8,128)} %reshape.158) | copy-start | bytes 7077892
  180.1 2.5 %copy-start.11 = (bf16[1,1,768,768]{3,2,1,0:T(8,128)(2,1)S(1)}, bf16[1,1,768,768]{3,2,1,0:T(8,128)(2,1)}, u32[]{:S(2)}) copy-start(bf16[1,1,768,768]{3,2,1,0:T(8,128)(2,1)} %param.15) | copy-start | bytes 3538948
